TPU v7x, 256 devices: a whole 4x4x8 slice. The times are simulated.
256 devices in a mesh: section: 2 (over core), req: 32 (over z, y), head: 4 (over x).
Axes of the slice: x: 4, y: 4, z: 8, core: 2. Of those that a mesh axis runs over, the one named last changes fastest.
Arguments:
- token_ids: int32 [128, 4], P('req'), may hold values from 0 to 31999
- request_order: int32 [128], replicated, may hold values from 0 to 127, each once
- window_lengths: int32 [128], replicated, may hold values from 1 to 512, as said below
- embed_table: bfloat16 [32000, 2048], P(('req', 'head')), may hold values from -6 to 6
- cache_arrived: bfloat16 [2, 128, 512, 2, 2048], P('section', None, 'req', None, 'head'), may hold values from -16 to 16
- state_arrived: float32 [2, 128, 128, 16, 128], P('section', None, 'req', 'head'), may hold values from -2 to 2
- conv_history: bfloat16 [2, 128, 3, 3, 2048], P('section', 'req', None, None, 'head'), may hold values from -6 to 6
- sink_cache: bfloat16 [2, 128, 4, 2, 2048], P('section', 'req', None, None, 'head'), may hold values from -16 to 16
- w_qkv: bfloat16 [2, 2048, 3, 2048], P('section', None, None, 'head'), may hold values from -0.125 to 0.125
- w_out: bfloat16 [2, 2048, 2048], P('section', 'head'), may hold values from -0.125 to 0.125
- w_beta: bfloat16 [2, 2048, 16], P('section', None, 'head'), may hold values from -0.125 to 0.125
- conv_taps: float32 [2, 4, 3, 2048], P('section', None, None, 'head'), may hold values from -3 to 3
- pre_gain: float32 [2, 2048], P('section'), may hold values from 0.25 to 1.75
- out_gain: float32 [2, 2048], P('section', 'head'), may hold values from 0.25 to 1.75
- score_scale_table: float32 [2, 16], P('section', 'head'), may hold values from 4 to 512
Outputs:
- layer_out: bfloat16 [2, 128, 4, 2048], P('section', 'req')
- final_state: float32 [2, 128, 128, 16, 128], P('section', 'req', None, 'head')
Inputs may be any that keep to these rules, and one draw needn't show every extreme that they name: `request_order`: a permutation of the arriving requests. `window_lengths`: some request holds a full window.
All inputs are finite; a program needn't handle non-finite values.
Results may differ from a plain program's by a relative error of at most 0.025.
Values may be sent and summed in bfloat16 or wider, within the bound.
No kernel may reach another device: no remote copies, remote signals or barrier semaphores. Data moves between devices by JAX's collectives and lax.ppermute only.
A program may use at most 128 MiB of HBM per device.

v0:
```python
import jax
import jax.numpy as jnp
from jax import lax
from jax.sharding import PartitionSpec as P

WIN = 512
epsilon = 1e-06
negative_big = -1e30


def passed_along(value, axis, by):
    peers = lax.axis_size(axis)
    pairs = [(i, i + by) for i in range(peers) if 0 <= i + by < peers]
    return lax.ppermute(value, axis, pairs)


def rms_scale(values, gain_row):
    return (
        values * lax.rsqrt(jnp.mean(values * values, axis=-1, keepdims=True) + epsilon) * gain_row
    )


def unit_rows(values):
    return values * lax.rsqrt(jnp.sum(values * values, axis=-1, keepdims=True) + epsilon)


def shards(
    token_ids,
    request_order,
    window_lengths,
    embed_table,
    cache_arrived,
    state_arrived,
    conv_history,
    sink_cache,
    w_qkv,
    w_out,
    w_beta,
    conv_taps,
    pre_gain,
    out_gain,
    score_scale_table,
):
    slot_count, token_count = token_ids.shape
    heads_dev = score_scale_table.shape[1]
    width = pre_gain.shape[1]
    local_width = out_gain.shape[1]
    head_dim = local_width // heads_dev
    group_index = lax.axis_index("req")
    section_index = lax.axis_index("section")
    vocab_dev = embed_table.shape[0]
    all_ids = lax.all_gather(token_ids, "req", axis=0, tiled=True)
    first_row = lax.axis_index(("req", "head")) * vocab_dev
    onehot = (
        all_ids.reshape(-1)[:, None] == first_row + jnp.arange(vocab_dev, dtype=jnp.int32)[None, :]
    ).astype(jnp.bfloat16)
    looked_up = jnp.dot(onehot, embed_table, preferred_element_type=jnp.float32)
    summed = lax.psum(looked_up, ("req", "head"))
    own_rows = lax.dynamic_slice_in_dim(
        summed, group_index * slot_count * token_count, slot_count * token_count, 0
    )
    embedded = own_rows.astype(jnp.bfloat16).reshape(slot_count, token_count, width)
    ordered_states = jnp.take(state_arrived, request_order, axis=1)
    delta_state = lax.all_to_all(ordered_states, "req", split_axis=1, concat_axis=2, tiled=True)[0]
    ordered_cache = jnp.take(cache_arrived, request_order, axis=1)
    all_lengths = jnp.take(window_lengths, request_order)
    own_lengths = lax.dynamic_slice_in_dim(all_lengths, group_index * slot_count, slot_count, 0)
    window_cache = lax.all_to_all(ordered_cache, "req", split_axis=1, concat_axis=2, tiled=True)[0]
    cache_rows = window_cache.shape[1]
    cache_holders = window_cache.shape[0]
    stored_key_rows = window_cache[:, :, 0].reshape(cache_holders, cache_rows, heads_dev, head_dim)
    cache_values = window_cache[:, :, 1].reshape(cache_holders, cache_rows, heads_dev, head_dim)
    sink_count = sink_cache.shape[2]
    anchor_key_rows = sink_cache[0][:, :, 0].reshape(slot_count, sink_count, heads_dev, head_dim)
    sink_values = sink_cache[0][:, :, 1].reshape(slot_count, sink_count, heads_dev, head_dim)
    qkv_matrix = w_qkv[0].reshape(width, 3 * local_width)
    conv_weights = conv_taps[0]
    softmax_scale_factor = score_scale_table[0]
    gain_head = out_gain[0].reshape(heads_dev, head_dim)
    new_index = jnp.arange(token_count, dtype=jnp.int32)
    row_index = jnp.arange(cache_rows, dtype=jnp.int32)
    history = conv_history[0]
    new_keys = jnp.zeros((slot_count, token_count, heads_dev, head_dim), jnp.bfloat16)
    new_values = jnp.zeros((slot_count, token_count, heads_dev, head_dim), jnp.bfloat16)
    received = jnp.zeros((slot_count, width), jnp.bfloat16)
    produced = jnp.zeros((slot_count, token_count, width), jnp.bfloat16)
    for position in range(token_count + 1):
        t_raw = position - section_index
        is_valid = (t_raw >= 0) & (t_raw < token_count)
        t_index = jnp.clip(t_raw, 0, token_count - 1)
        fresh_input = embedded[:, min(position, token_count - 1)]
        stream_in = jnp.where(section_index == 0, fresh_input, received)
        mixer_history = history
        mixer_delta_state = delta_state
        mixer_new_keys = new_keys
        mixer_new_values = new_values
        normed = rms_scale(stream_in.astype(jnp.float32), pre_gain[0]).astype(jnp.bfloat16)
        projected = (
            jnp.dot(normed, qkv_matrix, preferred_element_type=jnp.float32)
            .astype(jnp.bfloat16)
            .reshape(slot_count, 3, local_width)
        )
        conv_window = jnp.concatenate([mixer_history, projected[:, None]], axis=1)
        activated = jax.nn.silu(
            jnp.sum(conv_window.astype(jnp.float32) * conv_weights[None], axis=1)
        )
        query_vec = unit_rows(activated[:, 0].reshape(slot_count, heads_dev, head_dim))
        key_vec = unit_rows(activated[:, 1].reshape(slot_count, heads_dev, head_dim))
        value_vec = activated[:, 2].reshape(slot_count, heads_dev, head_dim)
        beta_gate = jax.nn.sigmoid(jnp.dot(normed, w_beta[0], preferred_element_type=jnp.float32))
        predicted = jnp.einsum(
            "skhv,shk->shv", mixer_delta_state, key_vec, precision=lax.Precision.HIGHEST
        )
        update = jnp.transpose(key_vec, (0, 2, 1))[:, :, :, None] * (value_vec - predicted)[:, None]
        mixer_delta_state = mixer_delta_state + beta_gate[:, None, :, None] * update
        readout = jnp.einsum(
            "skhv,shk->shv", mixer_delta_state, query_vec, precision=lax.Precision.HIGHEST
        )
        query_halfwidth = query_vec.astype(jnp.bfloat16)
        mixer_new_keys = lax.dynamic_update_slice_in_dim(
            mixer_new_keys, key_vec.astype(jnp.bfloat16)[:, None], t_index, 1
        )
        mixer_new_values = lax.dynamic_update_slice_in_dim(
            mixer_new_values, value_vec.astype(jnp.bfloat16)[:, None], t_index, 1
        )
        anchor_score_rows = (
            jnp.einsum(
                "kry,kgry->krg",
                query_halfwidth,
                anchor_key_rows,
                preferred_element_type=jnp.float32,
            )
            * softmax_scale_factor[None, :, None]
        )
        incoming_score_rows = (
            jnp.einsum(
                "kry,kgry->krg", query_halfwidth, mixer_new_keys, preferred_element_type=jnp.float32
            )
            * softmax_scale_factor[None, :, None]
        )
        fresh_mask = (new_index <= t_index)[None, None, :]
        home_max = jnp.maximum(
            jnp.max(anchor_score_rows, axis=-1),
            jnp.max(jnp.where(fresh_mask, incoming_score_rows, negative_big), axis=-1),
        )
        limit = jnp.maximum(WIN - own_lengths, t_index + 1)
        cache_mask = row_index[None, None, :] >= limit[:, None, None]
        stored_score_rows = (
            jnp.einsum(
                "xqa,xeqa->xqe",
                query_halfwidth,
                stored_key_rows,
                preferred_element_type=jnp.float32,
            )
            * softmax_scale_factor[None, :, None]
        )
        highest = jnp.maximum(
            home_max, jnp.max(jnp.where(cache_mask, stored_score_rows, negative_big), axis=-1)
        )
        cache_weights = jnp.where(cache_mask, jnp.exp(stored_score_rows - highest[:, :, None]), 0.0)
        cache_sum = jnp.sum(cache_weights, axis=-1)
        cache_part = jnp.einsum(
            "shw,swhd->shd",
            cache_weights.astype(jnp.bfloat16),
            cache_values,
            preferred_element_type=jnp.float32,
        )
        sink_weights = jnp.exp(anchor_score_rows - highest[:, :, None])
        fresh_weights = jnp.where(
            fresh_mask, jnp.exp(incoming_score_rows - highest[:, :, None]), 0.0
        )
        weight_sum = cache_sum + jnp.sum(sink_weights, axis=-1) + jnp.sum(fresh_weights, axis=-1)
        numerator = cache_part + jnp.einsum(
            "shj,sjhd->shd",
            sink_weights.astype(jnp.bfloat16),
            sink_values,
            preferred_element_type=jnp.float32,
        )
        numerator = numerator + jnp.einsum(
            "shj,sjhd->shd",
            fresh_weights.astype(jnp.bfloat16),
            mixer_new_values,
            preferred_element_type=jnp.float32,
        )
        attended = numerator / weight_sum[:, :, None]
        mixed_heads = (
            (rms_scale(readout, gain_head[None]) + attended)
            .astype(jnp.bfloat16)
            .reshape(slot_count, local_width)
        )
        partial_out = jnp.dot(mixed_heads, w_out[0], preferred_element_type=jnp.float32)
        mixer_out = lax.psum(partial_out, "head")
        stream_out = (stream_in.astype(jnp.float32) + mixer_out).astype(jnp.bfloat16)
        mixer_history = jnp.concatenate([mixer_history[:, 1:], projected[:, None]], axis=1)
        stream_out, next_history, next_state, next_keys, next_values = (
            stream_out,
            mixer_history,
            mixer_delta_state,
            mixer_new_keys,
            mixer_new_values,
        )
        history = jnp.where(is_valid, next_history, history)
        delta_state = jnp.where(is_valid, next_state, delta_state)
        new_keys = jnp.where(is_valid, next_keys, new_keys)
        new_values = jnp.where(is_valid, next_values, new_values)
        stored = lax.dynamic_update_slice_in_dim(produced, stream_out[:, None], t_index, 1)
        produced = jnp.where(is_valid, stored, produced)
        if position < token_count:
            received = passed_along(stream_out, "section", 1)
    return (produced[None], delta_state[None])


def solution(mesh):
    return jax.shard_map(
        shards,
        mesh=mesh,
        in_specs=(
            P("req", None),
            P(),
            P(),
            P(("req", "head"), None),
            P("section", None, "req", None, "head"),
            P("section", None, "req", "head", None),
            P("section", "req", None, None, "head"),
            P("section", "req", None, None, "head"),
            P("section", None, None, "head"),
            P("section", "head", None),
            P("section", None, "head"),
            P("section", None, None, "head"),
            P("section", None),
            P("section", "head"),
            P("section", "head"),
        ),
        out_specs=(P("section", "req", None, None), P("section", "req", None, "head", None)),
        check_vma=False,
    )
```

profile of v0, /device:TPU:2, one launch (start us, length us, event | category | flops | bytes accessed | tf_op | source)
XLA Modules:
  0.0 1202.1 jit_solution(7097759639940147544)
XLA Ops:
  3.7 2.4 gather_fusion
  7.4 11.5 all-to-all-start
  18.9 66.6 %all-gather = s32[32,4,4]{2,1,0:T(4,128)S(1)} all-gather(s32[1,4,4]{2,1,0:T(4,128)S(1)} %bitcast.617), channel_id=1, replica_groups=mesh['section'=2,'req'=32,'head'=4] {'req'}, dimensions={0}, use_global_device_ids=true | all-gather | bytes 2112 | tf_op jit(solution)/shard_map/all_gather | solution.py:52
  85.6 4.1 fusion.75
  89.7 3.2 copy.413
  92.9 5.1 gather_fusion.2
  98.0 4.7 fusion
  103.7 8.2 all-to-all-start.1
  111.9 792.8 %all-reduce.1 = bf16[512,2048]{1,0:T(8,128)(2,1)} all-reduce(f32[512,2048]{1,0:T(8,128)} %fusion.75), channel_id=1, replica_groups=mesh['section'=2,'req'=32,'head'=4] {'req','head'}, use_global_device_ids=true, to_apply=%region_0.0 | all-reduce | flops 1048576 | bytes 6291456 | tf_op jit(solution)/shard_map/psum | solution.py:58
  905.6 8.8 copy.140
  915.4 4.5 convolution_convert_fusion.4
  929.7 2.7 copy.144
  932.4 2.5 fusion.279
  934.9 4.2 copy.145
  939.1 2.0 fusion.214
  941.5 4.2 copy.146
  945.8 2.2 fusion.114
  948.7 20.5 %psum.43 = f32[4,2048]{1,0:T(4,128)S(1)} all-reduce(f32[4,2048]{1,0:T(4,128)S(1)} %fusion.9), channel_id=1, replica_groups=mesh['section'=2,'req'=32,'head'=4] {'head'}, use_global_device_ids=true, to_apply=%region_12.13 | all-reduce | flops 8192 | bytes 65536 | tf_op jit(solution)/shard_map/psum | solution.py:192
  969.9 2.0 collective-permute-start
  978.5 4.5 convolution_convert_fusion.3
  988.2 2.0 fusion.210
  992.0 1.9 convert_bitcast_fusion.4
  994.0 1.9 fusion.188
  997.7 2.1 fusion.42
  1000.6 2.1 fusion.35
  1005.6 15.6 %psum.44 = f32[4,2048]{1,0:T(4,128)} all-reduce(f32[4,2048]{1,0:T(4,128)} %fusion.7), channel_id=1, replica_groups=mesh['section'=2,'req'=32,'head'=4] {'head'}, use_global_device_ids=true, to_apply=%region_24.25 | all-reduce | flops 8192 | bytes 65536 | tf_op jit(solution)/shard_map/psum | solution.py:192
  1023.2 1.9 collective-permute-start.1
  1033.1 4.5 convolution_convert_fusion.2
  1044.1 2.0 fusion.206
  1050.8 1.9 fusion.190
  1055.3 2.2 fusion.271
  1057.8 2.7 fusion.33
  1062.5 16.8 %psum.45 = f32[4,2048]{1,0:T(4,128)} all-reduce(f32[4,2048]{1,0:T(4,128)S(1)} %fusion.5), channel_id=1, replica_groups=mesh['section'=2,'req'=32,'head'=4] {'head'}, use_global_device_ids=true, to_apply=%region_36.37 | all-reduce | flops 8192 | bytes 65536 | tf_op jit(solution)/shard_map/psum | solution.py:192
  1081.5 2.1 collective-permute-start.2
  1092.9 4.5 convolution_convert_fusion.1
  1101.9 2.0 fusion.202
  1107.1 1.9 convert_bitcast_fusion.2
  1109.0 1.9 fusion.192
  1112.9 2.5 fusion.80
  1115.6 3.4 fusion.31
  1121.9 15.6 %psum.46 = f32[4,2048]{1,0:T(4,128)} all-reduce(f32[4,2048]{1,0:T(4,128)} %fusion.3), channel_id=1, replica_groups=mesh['section'=2,'req'=32,'head'=4] {'head'}, use_global_device_ids=true, to_apply=%region_48.49 | all-reduce | flops 8192 | bytes 65536 | tf_op jit(solution)/shard_map/psum | solution.py:192
  1139.0 1.9 collective-permute-start.3
  1146.6 4.5 convolution_convert_fusion
  1156.2 2.0 fusion.198
  1166.7 3.6 fusion.39
  1172.0 3.4 fusion.26
  1177.1 16.8 %psum.47 = f32[4,2048]{1,0:T(4,128)} all-reduce(f32[4,2048]{1,0:T(4,128)S(1)} %fusion.1), channel_id=1, replica_groups=mesh['section'=2,'req'=32,'head'=4] {'head'}, use_global_device_ids=true, to_apply=%region_60.61 | all-reduce | flops 8192 | bytes 65536 | tf_op jit(solution)/shard_map/psum | solution.py:192
  1196.8 5.1 add_select_fusion
  (491 shorter events, 114.1 us)
Async XLA Ops:
  0.6 947.7 %copy-start = (bf16[1,512,2048]{2,1,0:T(8,128)(2,1)S(1)}, bf16[1,512,2048]{2,1,0:T(8,128)(2,1)}, u32[]{:S(2)}) copy-start(bf16[1,512,2048]{2,1,0:T(8,128)(2,1)} %param.24) | copy-start | bytes 6291460
  6.1 12.8 %copy-start.117 = (s32[4,4]{1,0:T(4,128)S(1)}, s32[4,4]{1,0:T(4,128)}, u32[]{:S(2)}) copy-start(s32[4,4]{1,0:T(4,128)} %param.15) | copy-start | bytes 196
  7.4 95.3 %all-to-all-start = ((f32[1,128,4,4,128]{4,3,2,0,1:T(4,128)}), f32[1,128,4,4,128]{4,3,2,0,1:T(4,128)S(1)}, u32[]{:S(2)}, u32[]{:S(2)}) async-start(f32[1,128,4,4,128]{4,3,2,0,1:T(4,128)} %bitcast_select_fusion.1), calls=%async_computation | async-start | bytes 2097152 | tf_op jit(solution)/shard_map/all_to_all | solution.py:64
  103.7 826.0 %all-to-all-start.1 = ((bf16[1,128,16,2,512]{4,2,3,0,1:T(8,128)(2,1)}), bf16[1,128,16,2,512]{4,2,3,0,1:T(8,128)(2,1)}, u32[]{:S(2)}, u32[]{:S(2)}) async-start(bf16[1,128,16,2,512]{4,2,3,0,1:T(8,128)(2,1)} %fusion), calls=%async_computation.1 | async-start | bytes 8388608 | tf_op jit(solution)/shard_map/all_to_all | solution.py:68
  111.8 792.8 %copy-start.11 = (bf16[1,4,3,3,512]{4,1,3,2,0:T(4,128)(2,1)S(1)}, bf16[1,4,3,3,512]{4,1,3,2,0:T(4,128)(2,1)}, u32[]{:S(2)}) copy-start(bf16[1,4,3,3,512]{4,1,3,2,0:T(4,128)(2,1)} %param.21) | copy-start | bytes 110596
  111.8 792.8 %copy-start.80 = (f32[1,4,3,512]{3,1,2,0:T(4,128)S(1)}, f32[1,4,3,512]{3,1,2,0:T(4,128)}, u32[]{:S(2)}) copy-start(f32[1,4,3,512]{3,1,2,0:T(4,128)} %param.26) | copy-start | bytes 73732
  905.6 9.7 copy-start.12
  915.3 6.7 copy-start.22
  915.3 7.3 copy-start.13
  915.3 9.7 copy-start.118
  922.2 7.4 copy-start.92
  922.2 25.9 %copy-start.87 = (bf16[4,4,512]{2,1,0:T(4,128)(2,1)}, bf16[4,4,512]{2,1,0:T(4,128)(2,1)S(1)}, u32[]{:S(2)}) copy-start(bf16[4,4,512]{2,1,0:T(4,128)(2,1)S(1)} %get-tuple-element.16) | copy-start | bytes 49156
  924.9 4.7 copy-start.34
  925.9 57.2 %copy-start.8 = (bf16[4,3,3,512]{3,0,2,1:T(4,128)(2,1)}, bf16[4,3,3,512]{3,0,2,1:T(4,128)(2,1)S(1)}, u32[]{:S(2)}) copy-start(bf16[4,3,3,512]{3,0,2,1:T(4,128)(2,1)S(1)} %maximum_select_fusion) | copy-start | bytes 110596
  969.9 7.7 collective-permute-start
  977.7 5.3 copy-start.16
  984.3 16.2 %copy-start.30 = (f32[4,4,128]{2,1,0:T(4,128)S(1)}, f32[4,4,128]{2,1,0:T(4,128)}, u32[]{:S(2)}) copy-start(f32[4,4,128]{2,1,0:T(4,128)} %copy-done.29) | copy-start | bytes 24580
  984.3 16.2 %copy-start.35 = (f32[4,128,4]{1,2,0:T(4,128)S(1)}, f32[4,128,4]{1,2,0:T(4,128)}, u32[]{:S(2)}) copy-start(f32[4,128,4]{1,2,0:T(4,128)} %copy-done.34) | copy-start | bytes 24580
  985.1 17.6 %copy-start.64 = (f32[4,128,4]{1,2,0:T(4,128)}, f32[4,128,4]{1,2,0:T(4,128)S(1)}, u32[]{:S(2)}) copy-start(f32[4,128,4]{1,2,0:T(4,128)S(1)} %fusion.317) | copy-start | bytes 24580
  987.3 9.8 copy-start.79
  997.7 5.1 copy-start.1
  997.7 5.2 copy-start.14
  1002.9 18.3 %slice-start = ((bf16[4,3,3,512]{3,0,2,1:T(4,128)(2,1)}), bf16[4,2,3,512]{3,0,2,1:T(4,128)(2,1)S(1)}, s32[]{:S(2)}) async-start(bf16[4,3,3,512]{3,0,2,1:T(4,128)(2,1)} %copy-done.8), calls=%async_computation.2 | async-start | bytes 49152 | tf_op jit(solution)/shard_map/slice | solution.py:194
  1002.9 18.3 %copy-start.25 = (bf16[4,1536]{1,0:T(4,128)(2,1)S(1)}, bf16[4,1536]{1,0:T(4,128)(2,1)}, u32[]{:S(2)}) copy-start(bf16[4,1536]{1,0:T(4,128)(2,1)} %copy-done.24) | copy-start | bytes 36868
  1023.2 7.5 collective-permute-start.1
  1025.8 4.9 copy-start.20
  1026.6 11.1 copy-start.21
  1031.6 6.0 copy-start.17
  1033.1 4.5 copy-start.10
  1037.7 17.7 %copy-start.31 = (f32[4,4,128]{2,1,0:T(4,128)S(1)}, f32[4,4,128]{2,1,0:T(4,128)}, u32[]{:S(2)}) copy-start(f32[4,4,128]{2,1,0:T(4,128)} %copy-done.29) | copy-start | bytes 24580
  1046.1 11.5 copy-start.36
  1080.1 17.3 %copy-start.9 = (bf16[4,3,3,512]{3,0,2,1:T(4,128)(2,1)}, bf16[4,3,3,512]{3,0,2,1:T(4,128)(2,1)S(1)}, u32[]{:S(2)}) copy-start(bf16[4,3,3,512]{3,0,2,1:T(4,128)(2,1)S(1)} %maximum_select_fusion.2) | copy-start | bytes 110596
  1081.5 8.9 collective-permute-start.2
  1091.3 6.0 copy-start.18
  1119.2 18.3 %slice-start.1 = ((bf16[4,3,3,512]{3,0,2,1:T(4,128)(2,1)}), bf16[4,2,3,512]{3,0,2,1:T(4,128)(2,1)S(1)}, s32[]{:S(2)}) async-start(bf16[4,3,3,512]{3,0,2,1:T(4,128)(2,1)} %copy-done.9), calls=%async_computation.3 | async-start | bytes 49152 | tf_op jit(solution)/shard_map/slice | solution.py:194
  1119.2 18.3 %copy-start.27 = (bf16[4,1536]{1,0:T(4,128)(2,1)S(1)}, bf16[4,1536]{1,0:T(4,128)(2,1)}, u32[]{:S(2)}) copy-start(bf16[4,1536]{1,0:T(4,128)(2,1)} %copy-done.26) | copy-start | bytes 36868
  1139.0 6.7 collective-permute-start.3
  1146.6 5.4 copy-start.19
  1151.1 9.4 copy-start.81
  1156.2 9.9 copy-start.78
  1166.7 5.3 copy-start.33
  1166.7 5.3 copy-start.38
  1166.7 5.3 copy-start.55
  1166.7 5.3 copy-start.58
  1166.7 5.3 copy-start.61
  1175.7 21.1 %copy-start.5 = (f32[1,4,32,4,4,128]{5,4,3,2,1,0:T(4,128)S(1)}, f32[1,4,32,4,4,128]{5,4,3,2,1,0:T(4,128)}, u32[]{:S(2)}) copy-start(f32[1,4,32,4,4,128]{5,4,3,2,1,0:T(4,128)} %copy.150) | copy-start | bytes 3145732
  1176.4 20.4 %copy-start.59 = (f32[4,4,128]{2,1,0:T(4,128)S(1)}, f32[4,4,128]{2,1,0:T(4,128)}, u32[]{:S(2)}) copy-start(f32[4,4,128]{2,1,0:T(4,128)} %copy-done.56) | copy-start | bytes 24580
  1176.4 20.4 %copy-start.62 = (f32[4,4,128]{2,1,0:T(4,128)S(1)}, f32[4,4,128]{2,1,0:T(4,128)}, u32[]{:S(2)}) copy-start(f32[4,4,128]{2,1,0:T(4,128)} %copy-done.60) | copy-start | bytes 24580
  (81 other events, 219.1 us)
where the time goes:
time: 1210 us; the launch traced here: 1200 us
  blocking collectives  945 us (78%)
  matrix products  81.3 us (7%)
  local copies, waits for them, and re-layouts  76.8 us (6%)
  other arithmetic  69.3 us (6%)
  starting transfers between devices  27.5 us (2%)
    psum x1, blocking collectives, shards(): summed = lax.psum(looked_up, ('req', 'head'))  793 us
    psum x5, blocking collectives, shards(): mixer_out = lax.psum(partial_out, 'head')  85.3 us
    all_gather x1, blocking collectives, shards(): all_ids = lax.all_gather(token_ids, 'req', axis=0, tiled=True)  66.6 us
  transfers between devices with their start and end apart: 6, of which 0 were waited for; matrix products, arithmetic and copies ran while one was open for 5% of the time, Pallas kernels for 0%

commit v1 on v0

--- a/solution.py
+++ b/solution.py
@@ -55,7 +55,7 @@
         all_ids.reshape(-1)[:, None] == first_row + jnp.arange(vocab_dev, dtype=jnp.int32)[None, :]
     ).astype(jnp.bfloat16)
     looked_up = jnp.dot(onehot, embed_table, preferred_element_type=jnp.float32)
-    summed = lax.psum(looked_up, ("req", "head"))
+    summed = lax.psum(lax.psum(looked_up, "req"), "head")
     own_rows = lax.dynamic_slice_in_dim(
         summed, group_index * slot_count * token_count, slot_count * token_count, 0
     )

time: 1210 us -> 641 us (0.53)
  blocking collectives: 945 us -> 206 us
  waiting for transfers between devices: 0.02 us -> 156 us
  between operations: 2.47 us -> 15.9 us
    psum x1, blocking collectives: 793 us -> 74.2 us  [shards(): summed = lax.psum(lax.psum(looked_up, 'req'), 'head')]
    psum x0 -> x1, waiting for transfers between devices: none -> 154 us  [shards(): summed = lax.psum(lax.psum(looked_up, 'req'), 'head')]
    all_gather x1, blocking collectives: 66.6 us -> 52.3 us  [shards(): all_ids = lax.all_gather(token_ids, 'req', axis=0, tiled=True)]
    unnamed x252 -> x248, local copies, waits for them, and re-layouts: 23.8 us -> 26.5 us
  transfers between devices with their start and end apart: 6 -> 7, of which waited for: 0 -> 2; matrix products, arithmetic and copies ran while one was open for 5% -> 11% of each run, Pallas kernels for 0% -> 0%
where the time goes in v1:
time: 641 us; the launch traced here: 629 us
  blocking collectives  206 us (32%)
  waiting for transfers between devices  156 us (24%)
  matrix products  82 us (13%)
  local copies, waits for them, and re-layouts  79.1 us (12%)
  other arithmetic  68.3 us (11%)
  starting transfers between devices  22.4 us (3%)
  between operations  15.9 us (2%)
    psum x1, waiting for transfers between devices, shards(): summed = lax.psum(lax.psum(looked_up, 'req'), 'head')  154 us
    psum x5, blocking collectives, shards(): mixer_out = lax.psum(partial_out, 'head')  79.2 us
    psum x1, blocking collectives, shards(): summed = lax.psum(lax.psum(looked_up, 'req'), 'head')  74.2 us
    all_gather x1, blocking collectives, shards(): all_ids = lax.all_gather(token_ids, 'req', axis=0, tiled=True)  52.3 us
    unnamed x248, local copies, waits for them, and re-layouts  26.5 us
    dot_general x5, matrix products, shards(): jnp.dot(normed, qkv_matrix, preferred_element_type=jnp.float32)  22.5 us
    dot_general x5, matrix products, shards(): jnp.einsum('skhv,shk->shv', mixer_delta_state, query_vec, precision=lax.P...  12.9 us
  transfers between devices with their start and end apart: 7, of which 2 were waited for; matrix products, arithmetic and copies ran while one was open for 11% of the time, Pallas kernels for 0%

profile of v1, /device:TPU:2, one launch (start us, length us, event | category | flops | bytes accessed | tf_op | source)
XLA Modules:
  0.0 629.0 jit_solution(11567480472478218798)
XLA Ops:
  7.2 52.3 %all-gather = s32[32,4,4]{2,1,0:T(4,128)S(1)} all-gather(s32[1,4,4]{2,1,0:T(4,128)} %bitcast.617), channel_id=1, replica_groups=mesh['section'=2,'req'=32,'head'=4] {'req'}, dimensions={0}, use_global_device_ids=true | all-gather | bytes 2112 | tf_op jit(solution)/shard_map/all_gather | solution.py:52
  59.6 4.1 fusion.75
  65.6 2.4 gather_fusion
  69.3 6.1 all-to-all-start
  75.6 5.3 copy.413
  80.8 5.1 gather_fusion.2
  85.9 8.8 %copy.140 = bf16[1,2048,3,512]{1,3,2,0:T(8,128)(2,1)} copy(bf16[1,2048,3,512]{3,1,2,0:T(8,128)(2,1)} %param.23) | data formatting | bytes 12582912 | tf_op args[8]
  99.1 4.7 fusion
  106.3 8.4 %all-to-all-start.1 = ((bf16[1,128,16,2,512]{4,2,3,0,1:T(8,128)(2,1)}), bf16[1,128,16,2,512]{4,2,3,0,1:T(8,128)(2,1)}, u32[]{:S(2)}, u32[]{:S(2)}) async-start(bf16[1,128,16,2,512]{4,2,3,0,1:T(8,128)(2,1)} %fusion), calls=%async_computation.1 | async-start | bytes 8388608 | tf_op jit(solution)/shard_map/all_to_all | solution.py:68
  117.9 154.1 %all-reduce.3.cloned.1.call-done = f32[512,2048]{1,0:T(8,128)} async-done(((f32[512,2048]{1,0:T(8,128)}), f32[512,2048]{1,0:T(8,128)}) %all-reduce.3.cloned.1.call-update) | async-done | bytes 4194320 | tf_op jit(solution)/shard_map/psum | solution.py:58
  272.0 74.2 %all-reduce.4 = bf16[512,2048]{1,0:T(8,128)(2,1)} all-reduce(f32[512,2048]{1,0:T(8,128)} %all-reduce.3.cloned.1.call-done), channel_id=1, replica_groups=mesh['section'=2,'req'=32,'head'=4] {'head'}, use_global_device_ids=true, to_apply=%region_1.0 | all-reduce | flops 1048576 | bytes 6291456 | tf_op jit(solution)/shard_map/psum | solution.py:58
  347.9 4.5 convolution_convert_fusion.4
  356.2 2.7 copy.144
  358.9 2.5 fusion.279
  361.4 4.2 copy.145
  365.5 2.0 fusion.214
  368.0 4.2 copy.146
  372.3 2.2 fusion.114
  375.2 14.0 %psum.51 = f32[4,2048]{1,0:T(4,128)S(1)} all-reduce(f32[4,2048]{1,0:T(4,128)S(1)} %fusion.9), channel_id=1, replica_groups=mesh['section'=2,'req'=32,'head'=4] {'head'}, use_global_device_ids=true, to_apply=%region_13.14 | all-reduce | flops 8192 | bytes 65536 | tf_op jit(solution)/shard_map/psum | solution.py:192
  389.9 2.0 collective-permute-start
  398.4 4.5 convolution_convert_fusion.3
  408.1 2.0 fusion.210
  411.9 1.9 convert_bitcast_fusion.4
  417.5 2.1 fusion.42
  420.4 2.1 fusion.35
  425.3 17.8 %psum.52 = f32[4,2048]{1,0:T(4,128)} all-reduce(f32[4,2048]{1,0:T(4,128)} %fusion.7), channel_id=1, replica_groups=mesh['section'=2,'req'=32,'head'=4] {'head'}, use_global_device_ids=true, to_apply=%region_25.26 | all-reduce | flops 8192 | bytes 65536 | tf_op jit(solution)/shard_map/psum | solution.py:192
  455.0 4.5 convolution_convert_fusion.2
  466.1 2.0 fusion.206
  472.6 1.9 fusion.190
  477.1 2.2 fusion.271
  479.5 2.7 fusion.33
  484.3 14.9 %psum.53 = f32[4,2048]{1,0:T(4,128)} all-reduce(f32[4,2048]{1,0:T(4,128)S(1)} %fusion.5), channel_id=1, replica_groups=mesh['section'=2,'req'=32,'head'=4] {'head'}, use_global_device_ids=true, to_apply=%region_37.38 | all-reduce | flops 8192 | bytes 65536 | tf_op jit(solution)/shard_map/psum | solution.py:192
  501.4 2.1 collective-permute-start.2
  512.8 4.5 convolution_convert_fusion.1
  521.8 2.0 fusion.202
  527.0 1.9 convert_bitcast_fusion.2
  528.9 1.9 fusion.192
  532.9 2.5 fusion.80
  535.5 3.4 fusion.31
  541.9 17.5 %psum.54 = f32[4,2048]{1,0:T(4,128)} all-reduce(f32[4,2048]{1,0:T(4,128)} %fusion.3), channel_id=1, replica_groups=mesh['section'=2,'req'=32,'head'=4] {'head'}, use_global_device_ids=true, to_apply=%region_49.50 | all-reduce | flops 8192 | bytes 65536 | tf_op jit(solution)/shard_map/psum | solution.py:192
  560.8 1.9 collective-permute-start.3
  568.5 4.5 convolution_convert_fusion
  578.0 2.0 fusion.198
  584.8 1.9 fusion.194
  588.6 3.6 fusion.39
  593.9 3.4 fusion.26
  599.0 14.9 %psum.55 = f32[4,2048]{1,0:T(4,128)} all-reduce(f32[4,2048]{1,0:T(4,128)S(1)} %fusion.1), channel_id=1, replica_groups=mesh['section'=2,'req'=32,'head'=4] {'head'}, use_global_device_ids=true, to_apply=%region_61.62 | all-reduce | flops 8192 | bytes 65536 | tf_op jit(solution)/shard_map/psum | solution.py:192
  616.8 5.1 add_select_fusion
  (490 shorter events, 117.6 us)
Async XLA Ops:
  7.2 367.7 %copy-start = (bf16[1,512,2048]{2,1,0:T(8,128)(2,1)S(1)}, bf16[1,512,2048]{2,1,0:T(8,128)(2,1)}, u32[]{:S(2)}) copy-start(bf16[1,512,2048]{2,1,0:T(8,128)(2,1)} %param.24) | copy-start | bytes 6291460
  7.2 264.8 %all-reduce.3.cloned.1.call-start = ((), (), s32[]{:S(2)}) async-start(), calls=%async_computation.2 | async-start | bytes 8388608 | tf_op jit(solution)/shard_map/psum | solution.py:58
  68.0 7.5 %copy-start.11 = (bf16[1,4,3,3,512]{4,1,3,2,0:T(4,128)(2,1)S(1)}, bf16[1,4,3,3,512]{4,1,3,2,0:T(4,128)(2,1)}, u32[]{:S(2)}) copy-start(bf16[1,4,3,3,512]{4,1,3,2,0:T(4,128)(2,1)} %param.21) | copy-start | bytes 110596
  68.0 7.5 %copy-start.79 = (f32[1,4,3,512]{3,1,2,0:T(4,128)S(1)}, f32[1,4,3,512]{3,1,2,0:T(4,128)}, u32[]{:S(2)}) copy-start(f32[1,4,3,512]{3,1,2,0:T(4,128)} %param.26) | copy-start | bytes 73732
  69.3 36.0 %all-to-all-start = ((f32[1,128,4,4,128]{4,3,2,0,1:T(4,128)}), f32[1,128,4,4,128]{4,3,2,0,1:T(4,128)S(1)}, u32[]{:S(2)}, u32[]{:S(2)}) async-start(f32[1,128,4,4,128]{4,3,2,0,1:T(4,128)} %bitcast_select_fusion.1), calls=%async_computation | async-start | bytes 2097152 | tf_op jit(solution)/shard_map/all_to_all | solution.py:64
  85.9 11.1 %copy-start.22 = (bf16[1,4,4,2,512]{4,3,2,1,0:T(2,128)(2,1)S(1)}, bf16[1,4,4,2,512]{4,3,2,1,0:T(2,128)(2,1)}, u32[]{:S(2)}) copy-start(bf16[1,4,4,2,512]{4,3,2,1,0:T(2,128)(2,1)} %param.22) | copy-start | bytes 98308
  97.1 258.6 %copy-start.91 = (bf16[4,4,512]{2,1,0:T(4,128)(2,1)}, bf16[4,4,512]{2,1,0:T(4,128)(2,1)S(1)}, u32[]{:S(2)}) copy-start(bf16[4,4,512]{2,1,0:T(4,128)(2,1)S(1)} %get-tuple-element.17) | copy-start | bytes 49156
  97.1 277.5 %copy-start.86 = (bf16[4,4,512]{2,1,0:T(4,128)(2,1)}, bf16[4,4,512]{2,1,0:T(4,128)(2,1)S(1)}, u32[]{:S(2)}) copy-start(bf16[4,4,512]{2,1,0:T(4,128)(2,1)S(1)} %get-tuple-element.16) | copy-start | bytes 49156
  106.3 249.9 %all-to-all-start.1 = ((bf16[1,128,16,2,512]{4,2,3,0,1:T(8,128)(2,1)}), bf16[1,128,16,2,512]{4,2,3,0,1:T(8,128)(2,1)}, u32[]{:S(2)}, u32[]{:S(2)}) async-start(bf16[1,128,16,2,512]{4,2,3,0,1:T(8,128)(2,1)} %fusion), calls=%async_computation.1 | async-start | bytes 8388608 | tf_op jit(solution)/shard_map/all_to_all | solution.py:68
  117.9 230.0 %copy-start.12 = (f32[1,2048]{1,0:T(1,128)S(1)}, f32[1,2048]{1,0:T(1,128)}, u32[]{:S(2)}) copy-start(f32[1,2048]{1,0:T(1,128)} %param.27) | copy-start | bytes 24580
  347.9 6.2 copy-start.117
  353.8 5.1 copy-start.28
  354.1 4.8 copy-start.33
  356.2 46.8 %copy-start.8 = (bf16[4,3,3,512]{3,0,2,1:T(4,128)(2,1)}, bf16[4,3,3,512]{3,0,2,1:T(4,128)(2,1)S(1)}, u32[]{:S(2)}) copy-start(bf16[4,3,3,512]{3,0,2,1:T(4,128)(2,1)S(1)} %maximum_select_fusion) | copy-start | bytes 110596
  389.9 6.2 collective-permute-start
  396.9 6.0 copy-start.16
  404.2 16.0 %copy-start.29 = (f32[4,4,128]{2,1,0:T(4,128)S(1)}, f32[4,4,128]{2,1,0:T(4,128)}, u32[]{:S(2)}) copy-start(f32[4,4,128]{2,1,0:T(4,128)} %copy-done.28) | copy-start | bytes 24580
  404.2 16.0 %copy-start.34 = (f32[4,128,4]{1,2,0:T(4,128)S(1)}, f32[4,128,4]{1,2,0:T(4,128)}, u32[]{:S(2)}) copy-start(f32[4,128,4]{1,2,0:T(4,128)} %copy-done.33) | copy-start | bytes 24580
  405.0 17.5 %copy-start.63 = (f32[4,128,4]{1,2,0:T(4,128)}, f32[4,128,4]{1,2,0:T(4,128)S(1)}, u32[]{:S(2)}) copy-start(f32[4,128,4]{1,2,0:T(4,128)S(1)} %fusion.317) | copy-start | bytes 24580
  407.2 9.7 %copy-start.78 = (f32[4,1,512]{2,0,1:T(4,128)S(1)}, f32[4,1,512]{2,0,1:T(4,128)}, u32[]{:S(2)}) copy-start(f32[4,1,512]{2,0,1:T(4,128)} %get-tuple-element.97) | copy-start | bytes 24580
  417.5 5.1 copy-start.2
  417.5 5.2 copy-start.14
  422.6 20.5 %slice-start = ((bf16[4,3,3,512]{3,0,2,1:T(4,128)(2,1)}), bf16[4,2,3,512]{3,0,2,1:T(4,128)(2,1)S(1)}, s32[]{:S(2)}) async-start(bf16[4,3,3,512]{3,0,2,1:T(4,128)(2,1)} %copy-done.8), calls=%async_computation.3 | async-start | bytes 49152 | tf_op jit(solution)/shard_map/slice | solution.py:194
  422.6 20.5 %copy-start.24 = (bf16[4,1536]{1,0:T(4,128)(2,1)S(1)}, bf16[4,1536]{1,0:T(4,128)(2,1)}, u32[]{:S(2)}) copy-start(bf16[4,1536]{1,0:T(4,128)(2,1)} %copy-done.23) | copy-start | bytes 36868
  445.1 7.5 %collective-permute-start.1 = (bf16[4,2048]{1,0:T(4,128)(2,1)}, bf16[4,2048]{1,0:T(4,128)(2,1)}, u32[]{:S(2)}, u32[]{:S(2)}) collective-permute-start(bf16[4,2048]{1,0:T(4,128)(2,1)} %get-tuple-element.57), channel_id=1, source_target_pairs={{0,128},{1,129},{2,130},{3,131},{4,132},{5,133},{6,134},{7,135},{8... | collective-permute-start | bytes 49160 | tf_op jit(solution)/shard_map/ppermute | solution.py:14
  447.8 4.9 copy-start.20
  448.5 11.1 %copy-start.21 = (bf16[2,4,8,128]{3,2,0,1:T(8,128)(2,1)}, bf16[2,4,8,128]{3,2,0,1:T(8,128)(2,1)S(1)}, u32[]{:S(2)}) copy-start(bf16[2,4,8,128]{3,2,0,1:T(8,128)(2,1)S(1)} %broadcast_select_fusion.5) | copy-start | bytes 49156
  453.5 6.0 copy-start.17
  455.0 4.5 copy-start.10
  459.6 17.5 %copy-start.30 = (f32[4,4,128]{2,1,0:T(4,128)S(1)}, f32[4,4,128]{2,1,0:T(4,128)}, u32[]{:S(2)}) copy-start(f32[4,4,128]{2,1,0:T(4,128)} %copy-done.28) | copy-start | bytes 24580
  468.0 11.3 %copy-start.35 = (f32[4,128,4]{1,2,0:T(4,128)S(1)}, f32[4,128,4]{1,2,0:T(4,128)}, u32[]{:S(2)}) copy-start(f32[4,128,4]{1,2,0:T(4,128)} %copy-done.33) | copy-start | bytes 24580
  500.0 17.3 %copy-start.9 = (bf16[4,3,3,512]{3,0,2,1:T(4,128)(2,1)}, bf16[4,3,3,512]{3,0,2,1:T(4,128)(2,1)S(1)}, u32[]{:S(2)}) copy-start(bf16[4,3,3,512]{3,0,2,1:T(4,128)(2,1)S(1)} %maximum_select_fusion.2) | copy-start | bytes 110596
  501.4 8.9 %collective-permute-start.2 = (bf16[4,2048]{1,0:T(4,128)(2,1)}, bf16[4,2048]{1,0:T(4,128)(2,1)}, u32[]{:S(2)}, u32[]{:S(2)}) collective-permute-start(bf16[4,2048]{1,0:T(4,128)(2,1)} %get-tuple-element.51), channel_id=1, source_target_pairs={{0,128},{1,129},{2,130},{3,131},{4,132},{5,133},{6,134},{7,135},{8... | collective-permute-start | bytes 49160 | tf_op jit(solution)/shard_map/ppermute | solution.py:14
  511.2 6.0 copy-start.18
  539.2 20.2 %slice-start.1 = ((bf16[4,3,3,512]{3,0,2,1:T(4,128)(2,1)}), bf16[4,2,3,512]{3,0,2,1:T(4,128)(2,1)S(1)}, s32[]{:S(2)}) async-start(bf16[4,3,3,512]{3,0,2,1:T(4,128)(2,1)} %copy-done.9), calls=%async_computation.4 | async-start | bytes 49152 | tf_op jit(solution)/shard_map/slice | solution.py:194
  539.2 20.2 %copy-start.26 = (bf16[4,1536]{1,0:T(4,128)(2,1)S(1)}, bf16[4,1536]{1,0:T(4,128)(2,1)}, u32[]{:S(2)}) copy-start(bf16[4,1536]{1,0:T(4,128)(2,1)} %copy-done.25) | copy-start | bytes 36868
  560.8 6.7 %collective-permute-start.3 = (bf16[4,2048]{1,0:T(4,128)(2,1)S(1)}, bf16[4,2048]{1,0:T(4,128)(2,1)}, u32[]{:S(2)}, u32[]{:S(2)}) collective-permute-start(bf16[4,2048]{1,0:T(4,128)(2,1)S(1)} %get-tuple-element.45), channel_id=1, source_target_pairs={{0,128},{1,129},{2,130},{3,131},{4,132},{5,133},{6,134},{7,135},{8... | collective-permute-start | bytes 49160 | tf_op jit(solution)/shard_map/ppermute | solution.py:14
  568.4 5.4 copy-start.19
  573.0 9.4 %copy-start.80 = (pred[4,512]{1,0:T(4,128)(4,1)S(1)}, pred[4,512]{1,0:T(4,128)(4,1)}, u32[]{:S(2)}) copy-start(pred[4,512]{1,0:T(4,128)(4,1)} %iota_compare_fusion) | copy-start | bytes 6148
  578.0 9.9 %copy-start.77 = (f32[4,1,512]{2,0,1:T(4,128)S(1)}, f32[4,1,512]{2,0,1:T(4,128)}, u32[]{:S(2)}) copy-start(f32[4,1,512]{2,0,1:T(4,128)} %get-tuple-element.88) | copy-start | bytes 24580
  588.6 5.3 copy-start.32
  588.6 5.3 copy-start.37
  588.6 5.3 copy-start.54
  588.6 5.3 copy-start.57
  588.6 5.3 copy-start.60
  597.6 19.2 %copy-start.6 = (f32[1,4,32,4,4,128]{5,4,3,2,1,0:T(4,128)S(1)}, f32[1,4,32,4,4,128]{5,4,3,2,1,0:T(4,128)}, u32[]{:S(2)}) copy-start(f32[1,4,32,4,4,128]{5,4,3,2,1,0:T(4,128)} %copy.150) | copy-start | bytes 3145732
  598.3 18.5 %copy-start.58 = (f32[4,4,128]{2,1,0:T(4,128)S(1)}, f32[4,4,128]{2,1,0:T(4,128)}, u32[]{:S(2)}) copy-start(f32[4,4,128]{2,1,0:T(4,128)} %copy-done.55) | copy-start | bytes 24580
  598.3 18.5 %copy-start.61 = (f32[4,4,128]{2,1,0:T(4,128)S(1)}, f32[4,4,128]{2,1,0:T(4,128)}, u32[]{:S(2)}) copy-start(f32[4,4,128]{2,1,0:T(4,128)} %copy-done.59) | copy-start | bytes 24580
  (80 other events, 209.2 us)
Sparse Core Ops, SparseCore 0:
  63.8 208.0 all-reduce.2
